TPU v7x, 256 devices: a whole 4x4x8 slice. The times are simulated.
256 devices in a mesh: pipe: 4 (over x), expert: 16 (over z, core), dp: 4 (over y).
Axes of the slice: x: 4, y: 4, z: 8, core: 2. Of those that a mesh axis runs over, the one named last changes fastest.
Arguments:
- inputs: bfloat16 [4, 8192, 4096], P('pipe', ('expert', 'dp')), may hold values from -6 to 6
- routes: int32 [4, 8192, 1], P('pipe', ('expert', 'dp')), may hold values from 0 to 15; in each aligned block of 128 rows (0 to 127, 128 to 255, ..., all dimensions but the last counted through in order) at most 10 rows name the same one
- router_scores: float32 [4, 8192, 8], P('pipe', ('expert', 'dp')), may hold values from -2 to 2
- cotangent: bfloat16 [4, 8192, 4096], P('pipe', ('expert', 'dp')), may hold values from -6 to 6
- w_gate: bfloat16 [4, 16, 768, 4096], P('pipe', 'expert', 'dp'), may hold values from -0.09375 to 0.09375
- w_up: bfloat16 [4, 16, 768, 4096], P('pipe', 'expert', 'dp'), may hold values from -0.09375 to 0.09375
- w_down: bfloat16 [4, 16, 768, 4096], P('pipe', 'expert', 'dp'), may hold values from -0.21875 to 0.21875
Outputs:
- score_grad: float32 [4, 8192, 8], P('pipe', ('expert', 'dp'))
- grad_prev: bfloat16 [4, 8192, 4096], P('pipe', ('expert', 'dp'))
- grad_gate: bfloat16 [4, 16, 768, 4096], P('pipe', 'expert', 'dp')
- grad_up: bfloat16 [4, 16, 768, 4096], P('pipe', 'expert', 'dp')
- grad_down: bfloat16 [4, 16, 768, 4096], P('pipe', 'expert', 'dp')
Inputs may be any that keep to these rules, and one draw needn't show every extreme that they name: `routes`: among the 128 tokens of one device in one section (one block) no expert is named more than 10 times, and in every draw some block names some expert exactly 10 times. Every expert is named by some token.
All inputs are finite; a program needn't handle non-finite values.
Results may differ from a plain program's by a relative error of at most 0.02.
Values may be sent and summed in bfloat16 or wider, within the bound.
No kernel may reach another device: no remote copies, remote signals or barrier semaphores. Data moves between devices by JAX's collectives and lax.ppermute only.
A program may use at most 128 MiB of HBM per device.

v0:
```python
import jax
import jax.numpy as jnp
from jax import lax
from jax.sharding import PartitionSpec as P


def from_behind(shard, axis, by):
    length = lax.axis_size(axis)
    pairs = [(i, i + by) for i in range(length) if 0 <= i + by < length]
    return lax.ppermute(shard, axis, pairs)


def route_tables(route_col, score_rows, experts, capacity):
    expert_ids = jnp.arange(experts, dtype=jnp.int32)
    onehot = (route_col[:, None] == expert_ids).astype(jnp.int32)
    earlier = jnp.cumsum(onehot, axis=0) - onehot
    slot = jnp.sum(onehot * earlier, axis=1)
    position = route_col * capacity + slot
    raised = jnp.exp(score_rows)
    weights = raised / jnp.sum(raised, axis=1, keepdims=True)
    gate = lax.optimization_barrier(weights[:, 0].astype(jnp.bfloat16)).astype(jnp.float32)
    table = position[:, None] == jnp.arange(experts * capacity, dtype=jnp.int32)
    return (weights, gate, table)


def per_device(inputs, routes, router_scores, cotangent, w_gate, w_up, w_down):
    tokens_in = inputs[0]
    upstream = cotangent[0]
    route_col = routes[0][:, 0]
    score_rows = router_scores[0]
    gate_mat = w_gate[0, 0]
    up_mat = w_up[0, 0]
    down_mat = w_down[0, 0]
    experts = lax.axis_size("expert")
    groups = lax.axis_size("dp")
    token_count, model_width = tokens_in.shape
    capacity = max(2, token_count * 5 // (4 * experts))
    weights, gate, table = route_tables(route_col, score_rows, experts, capacity)
    table_half = table.astype(jnp.bfloat16)
    token_contract = (((0,), (0,)), ((), ()))
    feature_contract = (((1,), (1,)), ((), ()))
    local_x = lax.dot_general(
        table_half, tokens_in, token_contract, preferred_element_type=jnp.float32
    )
    local_x = local_x.astype(jnp.bfloat16).reshape(experts, capacity, model_width)
    local_up = lax.dot_general(
        table_half, upstream, token_contract, preferred_element_type=jnp.float32
    )
    local_up = local_up.astype(jnp.bfloat16).reshape(experts, capacity, model_width)
    local_gate = jnp.sum(jnp.where(table, gate[:, None], jnp.float32(0.0)), axis=0)
    local_gate = local_gate.astype(jnp.bfloat16).reshape(experts, capacity)
    x_e = lax.all_to_all(local_x, "expert", 0, 0, tiled=True)
    up_e = lax.all_to_all(local_up, "expert", 0, 0, tiled=True)
    gate_e = lax.all_to_all(local_gate, "expert", 0, 0, tiled=True)
    rows_x = lax.all_gather(x_e, "dp", axis=0, tiled=True).reshape(-1, model_width)
    rows_up = lax.all_gather(up_e, "dp", axis=0, tiled=True).reshape(-1, model_width)
    rows_gate = lax.all_gather(gate_e, "dp", axis=0, tiled=True).reshape(-1)
    rows_grad = (rows_gate.astype(jnp.float32)[:, None] * rows_up.astype(jnp.float32)).astype(
        jnp.bfloat16
    )
    gate_pre = lax.dot_general(
        rows_x, gate_mat, feature_contract, preferred_element_type=jnp.float32
    )
    up_pre = lax.dot_general(rows_x, up_mat, feature_contract, preferred_element_type=jnp.float32)
    gate_sig = jax.nn.sigmoid(gate_pre)
    activated = (gate_pre * gate_sig * up_pre).astype(jnp.bfloat16)
    partial_out = jnp.dot(activated, down_mat, preferred_element_type=jnp.float32)
    row_score = jnp.sum(partial_out * rows_up.astype(jnp.float32), axis=1)
    row_score = lax.psum_scatter(
        row_score.reshape(groups, experts, capacity), "dp", scatter_dimension=0, tiled=True
    ).reshape(experts, capacity)
    slot_score = lax.all_to_all(row_score, "expert", 0, 0, tiled=True).reshape(-1)
    gate_grad = jnp.sum(jnp.where(table, slot_score[None, :], jnp.float32(0.0)), axis=1)
    is_first = (jnp.arange(score_rows.shape[1]) == 0).astype(jnp.float32)
    score_grad = gate_grad[:, None] * weights[:, 0:1] * (is_first - weights)
    hidden_grad = lax.dot_general(
        rows_grad, down_mat, feature_contract, preferred_element_type=jnp.float32
    )
    pre_gate = (hidden_grad * up_pre * gate_sig * (1.0 + gate_pre * (1.0 - gate_sig))).astype(
        jnp.bfloat16
    )
    pre_up = (hidden_grad * gate_pre * gate_sig).astype(jnp.bfloat16)
    grad_down = lax.dot_general(
        activated, rows_grad, token_contract, preferred_element_type=jnp.float32
    ).astype(jnp.bfloat16)
    grad_gate = lax.dot_general(
        pre_gate, rows_x, token_contract, preferred_element_type=jnp.float32
    ).astype(jnp.bfloat16)
    grad_up = lax.dot_general(
        pre_up, rows_x, token_contract, preferred_element_type=jnp.float32
    ).astype(jnp.bfloat16)
    partial_in = jnp.dot(pre_gate, gate_mat, preferred_element_type=jnp.float32)
    partial_in = partial_in + jnp.dot(pre_up, up_mat, preferred_element_type=jnp.float32)
    outgoing = partial_in.astype(jnp.bfloat16).reshape(groups, experts, capacity, model_width)
    summed = lax.psum_scatter(outgoing, "dp", scatter_dimension=0, tiled=True)
    summed = summed.reshape(experts, capacity, model_width)
    flat_in = lax.all_to_all(summed, "expert", 0, 0, tiled=True).reshape(-1, model_width)
    input_grad = jnp.dot(table_half, flat_in, preferred_element_type=jnp.float32).astype(
        jnp.bfloat16
    )
    handed = from_behind(input_grad, "pipe", -1)
    return (
        score_grad[None],
        handed[None],
        grad_gate[None, None],
        grad_up[None, None],
        grad_down[None, None],
    )


def solution(mesh):
    in_specs = (
        P("pipe", ("expert", "dp"), None),
        P("pipe", ("expert", "dp"), None),
        P("pipe", ("expert", "dp"), None),
        P("pipe", ("expert", "dp"), None),
        P("pipe", "expert", "dp", None),
        P("pipe", "expert", "dp", None),
        P("pipe", "expert", "dp", None),
    )
    out_specs = (
        P("pipe", ("expert", "dp"), None),
        P("pipe", ("expert", "dp"), None),
        P("pipe", "expert", "dp", None),
        P("pipe", "expert", "dp", None),
        P("pipe", "expert", "dp", None),
    )
    return jax.shard_map(
        per_device, mesh=mesh, in_specs=in_specs, out_specs=out_specs, check_vma=False
    )
```

profile of v0, /device:TPU:1, one launch (start us, length us, event | category | flops | bytes accessed | tf_op | source)
XLA Modules:
  0.0 496.6 jit_solution(5466417958805610884)
XLA Ops:
  7.2 0.8 fusion.18
  8.3 0.8 select_reduce_fusion.2
  9.1 0.7 multiply_add_fusion
  9.8 1.7 convolution_convert_fusion.2
  11.5 1.6 reshape.106
  13.1 61.0 %all_to_all.33 = bf16[16,10,4096]{2,1,0:T(8,128)(2,1)S(1)} all-to-all(bf16[16,10,4096]{2,1,0:T(8,128)(2,1)} %reshape.106), channel_id=1, replica_groups=mesh['pipe'=4,'expert'=16,'dp'=4] {'expert'}, dimensions={0} | all-to-all | bytes 2621440 | tf_op jit(solution)/shard_map/all_to_all | solution.py:53
  74.1 1.8 copy.38
  75.9 1.7 convolution_convert_fusion.3
  77.6 1.6 reshape.104
  79.2 53.9 %all_to_all.34 = bf16[16,10,4096]{2,1,0:T(8,128)(2,1)S(1)} all-to-all(bf16[16,10,4096]{2,1,0:T(8,128)(2,1)} %reshape.104), channel_id=1, replica_groups=mesh['pipe'=4,'expert'=16,'dp'=4] {'expert'}, dimensions={0} | all-to-all | bytes 2621440 | tf_op jit(solution)/shard_map/all_to_all | solution.py:52
  133.1 1.8 copy.36
  134.9 0.2 reduce-scatter.3.cloned.1.call-start
  135.2 12.2 %copy.39 = f32[64,10,4096]{2,1,0:T(8,128)} copy(bf16[64,10,4096]{2,0,1:T(8,128)(2,1)} %all-gather.6.cloned.1.call-done) | data formatting | bytes 15728640 | tf_op jit(solution)/shard_map/convert_element_type | solution.py:68
  147.4 12.4 %reshape.111 = f32[640,4096]{1,0:T(8,128)} reshape(f32[64,10,4096]{2,1,0:T(8,128)} %copy.39) | data formatting | bytes 20971520 | tf_op jit(solution)/shard_map/convert_element_type | solution.py:68
  159.7 35.0 %all-gather.4.cloned.1.call-done = bf16[64,10,4096]{2,0,1:T(8,128)(2,1)} async-done(((bf16[16,10,4096]{2,0,1:T(8,128)(2,1)}), bf16[64,10,4096]{2,0,1:T(8,128)(2,1)}) %all-gather.4.cloned.1.call-update) | async-done | bytes 5242896 | tf_op jit(solution)/shard_map/all_gather | solution.py:55
  194.7 8.9 %copy.37 = bf16[64,10,4096]{2,1,0:T(8,128)(2,1)} copy(bf16[64,10,4096]{2,0,1:T(8,128)(2,1)} %all-gather.4.cloned.1.call-done) | data formatting | bytes 10485760 | tf_op jit(solution)/shard_map/all_gather | solution.py:55
  203.7 8.7 %reshape.105 = bf16[640,4096]{1,0:T(8,128)(2,1)} reshape(bf16[64,10,4096]{2,1,0:T(8,128)(2,1)} %copy.37) | data formatting | bytes 10485760 | tf_op jit(solution)/shard_map/reshape | solution.py:55
  212.4 4.5 fusion.14
  217.0 4.6 multiply_convert_fusion.9
  221.6 1.8 multiply_reduce_fusion
  223.4 0.8 reshape.107
  224.2 21.3 %reduce-scatter.3.cloned.1.call-done = f32[1,16,10]{2,1,0:T(8,128)} async-done(((f32[4,16,10]{2,1,0:T(8,128)}), f32[1,16,10]{2,1,0:T(8,128)}) %reduce-scatter.3.cloned.1.call-update) | async-done | bytes 656 | tf_op jit(solution)/shard_map/reduce_scatter | solution.py:69
  245.5 9.9 %all-to-all-start.2 = ((f32[16,1,10]{2,1,0:T(1,128)}), f32[16,1,10]{2,1,0:T(1,128)S(1)}, u32[]{:S(2)}, u32[]{:S(2)}) async-start(f32[16,1,10]{2,1,0:T(1,128)} %bitcast.68), calls=%async_computation.3 | async-start | bytes 16384 | tf_op jit(solution)/shard_map/all_to_all | solution.py:72
  255.4 0.3 reduce-scatter.5.cloned.1.call-start
  255.7 6.7 %all-to-all-done.2 = f32[16,1,10]{2,1,0:T(1,128)S(1)} async-done(((f32[16,1,10]{2,1,0:T(1,128)}), f32[16,1,10]{2,1,0:T(1,128)S(1)}, u32[]{:S(2)}, u32[]{:S(2)}) %all-to-all-start.2) | async-done | bytes 672 | tf_op jit(solution)/shard_map/all_to_all | solution.py:72
  262.4 0.5 broadcast.42
  262.9 0.7 reduce.4
  264.0 10.1 %all_to_all.35 = bf16[16,1,10]{2,1,0:T(2,128)(2,1)S(1)} all-to-all(bf16[16,1,10]{2,1,0:T(2,128)(2,1)S(1)} %convert_element_type.125), channel_id=1, replica_groups=mesh['pipe'=4,'expert'=16,'dp'=4] {'expert'}, dimensions={0} | all-to-all | bytes 640 | tf_op jit(solution)/shard_map/all_to_all | solution.py:54
  274.1 9.0 %all-gather = bf16[64,1,10]{2,0,1:T(8,128)(2,1)S(1)} all-gather(bf16[16,1,10]{2,0,1:T(8,128)(2,1)S(1)} %copy.42), channel_id=2, replica_groups=mesh['pipe'=4,'expert'=16,'dp'=4] {'dp'}, dimensions={0}, use_global_device_ids=true | all-gather | bytes 1600 | tf_op jit(solution)/shard_map/all_gather | solution.py:57
  283.2 4.5 multiply_convert_fusion.1
  287.7 6.4 %copy.44 = bf16[64,10,4096]{2,1,0:T(8,128)(2,1)} copy(bf16[64,10,4096]{2,0,1:T(8,128)(2,1)S(1)} %multiply_convert_fusion.1) | data formatting | bytes 10485760 | tf_op jit(solution)/shard_map/convert_element_type | solution.py:58
  294.1 8.7 %convert_element_type.110 = bf16[640,4096]{1,0:T(8,128)(2,1)} reshape(bf16[64,10,4096]{2,1,0:T(8,128)(2,1)} %copy.44) | data formatting | bytes 10485760 | tf_op jit(solution)/shard_map/convert_element_type | solution.py:58
  302.8 5.0 %multiply_convert_fusion.7 = (bf16[640,192]{0,1:T(8,128)(2,1)S(1)}, bf16[640,192]{0,1:T(8,128)(2,1)S(1)}) fusion(f32[640,192]{0,1:T(8,128)S(1)} %copy-done.8, f32[640,192]{0,1:T(8,128)S(1)} %get-tuple-element.10, bf16[640,4096]{1,0:T(8,128)(2,1)} %convert_element_type.110, bf16[1,1,192,4096]{3,2,1,0:T(8,128)(2,1)} %param.13), kind=kOutput, calls=%fused_computation.27 | convolution fusion | flops 1008230400 | bytes 8290304 | tf_op jit(solution)/shard_map/dot_general | solution.py:76
  307.9 1.6 fusion.12
  309.4 4.0 add_convert_fusion
  313.5 8.2 %reshape.108 = bf16[4,16,10,4096]{3,2,1,0:T(8,128)(2,1)} reshape(bf16[640,4096]{1,0:T(8,128)(2,1)} %add_convert_fusion) | data formatting | bytes 10485760 | tf_op jit(solution)/shard_map/reshape | solution.py:94
  321.7 80.8 %reduce-scatter.5.cloned.1.call-done = bf16[1,16,10,4096]{3,2,1,0:T(8,128)(2,1)} async-done(((bf16[4,16,10,4096]{3,2,1,0:T(8,128)(2,1)}), bf16[1,16,10,4096]{3,2,1,0:T(8,128)(2,1)}) %reduce-scatter.5.cloned.1.call-update) | async-done | bytes 1310736 | tf_op jit(solution)/shard_map/reduce_scatter | solution.py:95
  402.5 7.6 %all-to-all-start.4 = ((bf16[16,10,4096]{2,1,0:T(8,128)(2,1)}), bf16[16,10,4096]{2,1,0:T(8,128)(2,1)}, u32[]{:S(2)}, u32[]{:S(2)}) async-start(bf16[16,10,4096]{2,1,0:T(8,128)(2,1)} %bitcast.66), calls=%async_computation.6 | async-start | bytes 4194304 | tf_op jit(solution)/shard_map/all_to_all | solution.py:97
  410.1 0.7 subtract_multiply_fusion
  410.8 48.4 %all-to-all-done.4 = bf16[16,10,4096]{2,1,0:T(8,128)(2,1)} async-done(((bf16[16,10,4096]{2,1,0:T(8,128)(2,1)}), bf16[16,10,4096]{2,1,0:T(8,128)(2,1)}, u32[]{:S(2)}, u32[]{:S(2)}) %all-to-all-start.4) | async-done | bytes 1310752 | tf_op jit(solution)/shard_map/all_to_all | solution.py:97
  459.2 1.8 reshape.110
  461.0 1.5 convolution_convert_fusion.4
  462.4 1.7 collective-permute-start
  464.1 5.0 %fusion.4 = bf16[1,1,192,4096]{3,2,1,0:T(8,128)(2,1)} fusion(bf16[640,192]{0,1:T(8,128)(2,1)S(1)} %get-tuple-element.8, bf16[640,4096]{1,0:T(8,128)(2,1)} %reshape.105), kind=kOutput, calls=%fused_computation.13 | convolution fusion | flops 1007419392 | bytes 7061504 | tf_op jit(solution)/shard_map/dot_general | solution.py:86
  469.3 5.0 %fusion.5 = bf16[1,1,192,4096]{3,2,1,0:T(8,128)(2,1)} fusion(bf16[640,192]{0,1:T(8,128)(2,1)S(1)} %copy-done.2, bf16[640,4096]{1,0:T(8,128)(2,1)} %reshape.105), kind=kOutput, calls=%fused_computation.14 | convolution fusion | flops 1007419392 | bytes 7061504 | tf_op jit(solution)/shard_map/dot_general | solution.py:89
  474.3 6.6 %fusion.3 = bf16[1,1,192,4096]{3,2,1,0:T(8,128)(2,1)} fusion(bf16[640,192]{0,1:T(8,128)(2,1)S(1)} %get-tuple-element.9, f32[640,4096]{1,0:T(8,128)} %reshape.111, f32[640]{0:T(1024)S(1)} %reshape.112), kind=kOutput, calls=%fused_computation.12 | convolution fusion | flops 1012662272 | bytes 12306944 | tf_op jit(solution)/shard_map/dot_general | solution.py:83
  480.9 8.2 %collective-permute-done = bf16[128,4096]{1,0:T(8,128)(2,1)S(1)} collective-permute-done((bf16[128,4096]{1,0:T(8,128)(2,1)}, bf16[128,4096]{1,0:T(8,128)(2,1)S(1)}, u32[]{:S(2)}, u32[]{:S(2)}) %collective-permute-start) | collective-permute-done | bytes 1048608 | tf_op jit(solution)/shard_map/ppermute | solution.py:10
  489.1 1.0 copy.46
  (46 shorter events, 1.0 us)
Async XLA Ops:
  7.2 209.8 %copy-start = (bf16[1,1,192,4096]{3,2,1,0:T(8,128)(2,1)S(1)}, bf16[1,1,192,4096]{3,2,1,0:T(8,128)(2,1)}, u32[]{:S(2)}) copy-start(bf16[1,1,192,4096]{3,2,1,0:T(8,128)(2,1)} %param.12) | copy-start | bytes 4718596
  7.2 128.0 %all-gather.6.cloned.1.call-start = ((), (), s32[]{:S(2)}) async-start(), calls=%async_computation.8 | async-start | bytes 6553600 | tf_op jit(solution)/shard_map/all_gather | solution.py:56
  75.9 118.9 %all-gather.4.cloned.1.call-start = ((), (), s32[]{:S(2)}) async-start(), calls=%async_computation.7 | async-start | bytes 6553600 | tf_op jit(solution)/shard_map/all_gather | solution.py:55
  133.1 2.0 copy-start.6
  134.9 110.6 %reduce-scatter.3.cloned.1.call-start = ((), (), s32[]{:S(2)}) async-start(), calls=%async_computation.9 | async-start | bytes 40960 | tf_op jit(solution)/shard_map/reduce_scatter | solution.py:69
  203.7 8.7 %copy-start.4 = (bf16[1,1,192,4096]{3,2,1,0:T(8,128)(2,1)S(1)}, bf16[1,1,192,4096]{3,2,1,0:T(8,128)(2,1)}, u32[]{:S(2)}) copy-start(bf16[1,1,192,4096]{3,2,1,0:T(8,128)(2,1)} %param.11) | copy-start | bytes 4718596
  212.4 9.2 %slice-start = ((s8[10485760]{0:T(1024)(128)(4,1)}), s8[4194304]{0:T(1024)(128)(4,1)S(1)}, s32[]{:S(2)}) async-start(s8[10485760]{0:T(1024)(128)(4,1)} %bitcast.64), calls=%async_computation.11 | async-start | bytes 8388608
  212.4 9.2 %slice-start.1 = ((s8[10485760]{0:T(1024)(128)(4,1)}), s8[4194304]{0:T(1024)(128)(4,1)S(1)}, s32[]{:S(2)}) async-start(s8[10485760]{0:T(1024)(128)(4,1)} %bitcast.64), calls=%async_computation.12 | async-start | bytes 8388608
  216.9 4.6 copy-start.7
  216.9 4.6 slice-start.2
  216.9 4.6 copy-start.3
  245.5 16.9 %all-to-all-start.2 = ((f32[16,1,10]{2,1,0:T(1,128)}), f32[16,1,10]{2,1,0:T(1,128)S(1)}, u32[]{:S(2)}, u32[]{:S(2)}) async-start(f32[16,1,10]{2,1,0:T(1,128)} %bitcast.68), calls=%async_computation.3 | async-start | bytes 16384 | tf_op jit(solution)/shard_map/all_to_all | solution.py:72
  255.4 147.1 %reduce-scatter.5.cloned.1.call-start = ((), (), s32[]{:S(2)}) async-start(), calls=%async_computation.10 | async-start | bytes 10485760 | tf_op jit(solution)/shard_map/reduce_scatter | solution.py:95
  294.1 8.7 %copy-start.8 = (f32[640,192]{0,1:T(8,128)S(1)}, f32[640,192]{0,1:T(8,128)}, u32[]{:S(2)}) copy-start(f32[640,192]{0,1:T(8,128)} %copy-done.7) | copy-start | bytes 1474564
  302.8 5.0 %copy-start.5 = (bf16[1,1,192,4096]{3,2,1,0:T(8,128)(2,1)S(1)}, bf16[1,1,192,4096]{3,2,1,0:T(8,128)(2,1)}, u32[]{:S(2)}) copy-start(bf16[1,1,192,4096]{3,2,1,0:T(8,128)(2,1)} %param.11) | copy-start | bytes 4718596
  307.8 1.6 copy-start.1
  402.5 56.7 %all-to-all-start.4 = ((bf16[16,10,4096]{2,1,0:T(8,128)(2,1)}), bf16[16,10,4096]{2,1,0:T(8,128)(2,1)}, u32[]{:S(2)}, u32[]{:S(2)}) async-start(bf16[16,10,4096]{2,1,0:T(8,128)(2,1)} %bitcast.66), calls=%async_computation.6 | async-start | bytes 4194304 | tf_op jit(solution)/shard_map/all_to_all | solution.py:97
  462.4 6.9 %copy-start.2 = (bf16[640,192]{0,1:T(8,128)(2,1)S(1)}, bf16[640,192]{0,1:T(8,128)(2,1)}, u32[]{:S(2)}) copy-start(bf16[640,192]{0,1:T(8,128)(2,1)} %copy-done.1) | copy-start | bytes 737284
  462.4 26.6 %collective-permute-start = (bf16[128,4096]{1,0:T(8,128)(2,1)}, bf16[128,4096]{1,0:T(8,128)(2,1)S(1)}, u32[]{:S(2)}, u32[]{:S(2)}) collective-permute-start(bf16[128,4096]{1,0:T(8,128)(2,1)} %convolution_convert_fusion.4), channel_id=1, source_target_pairs={{64,0},{128,64},{192,128},{65,1},{129,65},{193,129},{66,2},{130,66... | collective-permute-start | bytes 3145736 | tf_op jit(solution)/shard_map/ppermute | solution.py:10
Sparse Core Ops, SparseCore 0:
  76.0 56.2 all-gather.5
  135.1 59.6 all-gather.3
  224.3 21.1 reduce-scatter.2
  321.8 80.6 reduce-scatter.4
where the time goes:
time: 498 us; the launch traced here: 497 us
  waiting for transfers between devices  200 us (40%)
  blocking collectives  134 us (27%)
  local copies, waits for them, and re-layouts  76.7 us (15%)
  matrix products  43 us (9%)
  starting transfers between devices  19.8 us (4%)
  between operations  14.1 us (3%)
  other arithmetic  8.57 us (2%)
    reduce_scatter x1, waiting for transfers between devices, per_device(): summed = lax.psum_scatter(outgoing, 'dp', scatter_dimension=0, tiled=True)  80.8 us
    all_to_all x1, blocking collectives, per_device(): up_e = lax.all_to_all(local_up, 'expert', 0, 0, tiled=True)  61 us
    all_to_all x1, blocking collectives, per_device(): x_e = lax.all_to_all(local_x, 'expert', 0, 0, tiled=True)  53.9 us
    all_to_all x1, waiting for transfers between devices, per_device(): lax.all_to_all(summed, 'expert', 0, 0, tiled=True).reshape(-1, model_width)  48.4 us
    all_gather x1, waiting for transfers between devices, per_device(): lax.all_gather(x_e, 'dp', axis=0, tiled=True).reshape(-1, model_width)  35 us
    convert_element_type x2, local copies, waits for them, and re-layouts, per_device(): row_score = jnp.sum(partial_out * rows_up.astype(jnp.float32), axis=1)  24.5 us
    reduce_scatter x1, waiting for transfers between devices, per_device(): lax.psum_scatter(row_score.reshape(groups, experts, capacity), 'dp', scat...  21.3 us
    convert_element_type x2, local copies, waits for them, and re-layouts, per_device(): (rows_gate.astype(jnp.float32)[:, None] * rows_up.astype(jnp.float32)).as...  15.1 us
  transfers between devices with their start and end apart: 7, of which 6 were waited for; matrix products, arithmetic and copies ran while one was open for 9% of the time, Pallas kernels for 0%

commit v1 on v0

--- a/solution.py
+++ b/solution.py
@@ -2,6 +2,13 @@
 import jax.numpy as jnp
 from jax import lax
 from jax.sharding import PartitionSpec as P
+
+
+def exchange_gather(x, axis, dim):
+    size = lax.axis_size(axis)
+    tiles = jnp.stack([x for _ in range(size)])
+    tiles = lax.all_to_all(tiles, axis, split_axis=0, concat_axis=0)
+    return jnp.concatenate(tiles, axis=dim)
 
 
 def from_behind(shard, axis, by):
@@ -52,7 +59,7 @@
     x_e = lax.all_to_all(local_x, "expert", 0, 0, tiled=True)
     up_e = lax.all_to_all(local_up, "expert", 0, 0, tiled=True)
     gate_e = lax.all_to_all(local_gate, "expert", 0, 0, tiled=True)
-    rows_x = lax.all_gather(x_e, "dp", axis=0, tiled=True).reshape(-1, model_width)
+    rows_x = exchange_gather(x_e, "dp", 0).reshape(-1, model_width)
     rows_up = lax.all_gather(up_e, "dp", axis=0, tiled=True).reshape(-1, model_width)
     rows_gate = lax.all_gather(gate_e, "dp", axis=0, tiled=True).reshape(-1)
     rows_grad = (rows_gate.astype(jnp.float32)[:, None] * rows_up.astype(jnp.float32)).astype(

time: 498 us -> 526 us (1.056)
  waiting for transfers between devices: 200 us -> 220 us
    all_to_all x0 -> x1, waiting for transfers between devices: none -> 59.5 us  [exchange_gather(): tiles = lax.all_to_all(tiles, axis, split_axis=0, concat_axis=0)]
    all_gather x1 -> x0, waiting for transfers between devices: 35 us -> none  [per_device(): lax.all_gather(x_e, 'dp', axis=0, tiled=True).reshape(-1, model_width)]
    another operation x0 -> x2, local copies, waits for them, and re-layouts: none -> 11.7 us  [the longest x1 8.78 us: per_device(): rows_x = exchange_gather(x_e, 'dp', 0).reshape(-1, model_width)]
    all_to_all x0 -> x1, local copies, waits for them, and re-layouts: none -> 9.1 us  [exchange_gather(): tiles = lax.all_to_all(tiles, axis, split_axis=0, concat_axis=0)]
    all_gather x1 -> x0, local copies, waits for them, and re-layouts: 8.94 us -> none  [per_device(): lax.all_gather(x_e, 'dp', axis=0, tiled=True).reshape(-1, model_width)]
    reshape x1 -> x0, local copies, waits for them, and re-layouts: 8.72 us -> none  [per_device(): lax.all_gather(x_e, 'dp', axis=0, tiled=True).reshape(-1, model_width)]
where the time goes in v1:
time: 526 us; the launch traced here: 525 us
  waiting for transfers between devices  220 us (42%)
  blocking collectives  134 us (25%)
  local copies, waits for them, and re-layouts  78.7 us (15%)
  matrix products  44.6 us (8%)
  starting transfers between devices  25 us (5%)
  between operations  14 us (3%)
  other arithmetic  8.57 us (2%)
    reduce_scatter x1, waiting for transfers between devices, per_device(): summed = lax.psum_scatter(outgoing, 'dp', scatter_dimension=0, tiled=True)  80.8 us
    all_to_all x1, blocking collectives, per_device(): up_e = lax.all_to_all(local_up, 'expert', 0, 0, tiled=True)  61 us
    all_to_all x1, waiting for transfers between devices, exchange_gather(): tiles = lax.all_to_all(tiles, axis, split_axis=0, concat_axis=0)  59.5 us
    all_to_all x1, blocking collectives, per_device(): x_e = lax.all_to_all(local_x, 'expert', 0, 0, tiled=True)  53.9 us
    all_to_all x1, waiting for transfers between devices, per_device(): lax.all_to_all(summed, 'expert', 0, 0, tiled=True).reshape(-1, model_width)  48.4 us
    convert_element_type x2, local copies, waits for them, and re-layouts, per_device(): row_score = jnp.sum(partial_out * rows_up.astype(jnp.float32), axis=1)  23.7 us
    reduce_scatter x1, waiting for transfers between devices, per_device(): lax.psum_scatter(row_score.reshape(groups, experts, capacity), 'dp', scat...  16.4 us
    convert_element_type x2, local copies, waits for them, and re-layouts, per_device(): (rows_gate.astype(jnp.float32)[:, None] * rows_up.astype(jnp.float32)).as...  15.1 us
  transfers between devices with their start and end apart: 7, of which 6 were waited for; matrix products, arithmetic and copies ran while one was open for 9% of the time, Pallas kernels for 0%

profile of v1, /device:TPU:1, one launch (start us, length us, event | category | flops | bytes accessed | tf_op | source)
XLA Modules:
  0.0 525.0 jit_solution(10714696820215009246)
XLA Ops:
  7.2 0.8 fusion.18
  8.3 0.8 select_reduce_fusion.2
  9.1 0.7 multiply_add_fusion
  9.8 1.7 convolution_convert_fusion.2
  11.5 1.6 reshape.104
  13.1 61.0 %all_to_all.38 = bf16[16,10,4096]{2,1,0:T(8,128)(2,1)S(1)} all-to-all(bf16[16,10,4096]{2,1,0:T(8,128)(2,1)} %reshape.104), channel_id=1, replica_groups=mesh['pipe'=4,'expert'=16,'dp'=4] {'expert'}, dimensions={0} | all-to-all | bytes 2621440 | tf_op jit(solution)/shard_map/all_to_all | solution.py:60
  74.1 1.8 copy.38
  75.9 1.7 convolution_convert_fusion.3
  77.6 1.6 reshape.103
  79.2 53.9 %all_to_all.39 = bf16[16,10,4096]{2,1,0:T(8,128)(2,1)S(1)} all-to-all(bf16[16,10,4096]{2,1,0:T(8,128)(2,1)} %reshape.103), channel_id=1, replica_groups=mesh['pipe'=4,'expert'=16,'dp'=4] {'expert'}, dimensions={0} | all-to-all | bytes 2621440 | tf_op jit(solution)/shard_map/all_to_all | solution.py:59
  133.1 0.7 copy.36
  133.8 2.9 stack.2
  136.7 5.2 all-to-all-start.1
  142.3 59.5 %all-to-all-done.1 = bf16[4,16,10,4096]{3,1,2,0:T(8,128)(2,1)} async-done(((bf16[4,16,10,4096]{3,1,2,0:T(8,128)(2,1)}), bf16[4,16,10,4096]{3,1,2,0:T(8,128)(2,1)}, u32[]{:S(2)}, u32[]{:S(2)}) %all-to-all-start.1) | async-done | bytes 5242912 | tf_op jit(solution)/shard_map/all_to_all | solution.py:10
  201.8 9.1 %copy.37 = bf16[4,16,10,4096]{3,2,1,0:T(8,128)(2,1)} copy(bf16[4,16,10,4096]{3,1,2,0:T(8,128)(2,1)} %all-to-all-done.1) | data formatting | bytes 10485760 | tf_op jit(solution)/shard_map/all_to_all | solution.py:10
  210.9 8.8 %reshape_reshape.3 = bf16[640,4096]{1,0:T(8,128)(2,1)} reshape(bf16[4,16,10,4096]{3,2,1,0:T(8,128)(2,1)} %copy.37) | data formatting | bytes 10485760 | tf_op jit(solution)/shard_map/reshape;reshape | solution.py:62
  219.6 4.5 fusion.14
  224.2 0.8 copy-done.7
  224.9 1.9 multiply_convert_fusion.9
  226.9 11.9 %copy.39 = f32[64,10,4096]{2,1,0:T(8,128)} copy(bf16[64,10,4096]{2,0,1:T(8,128)(2,1)} %all-gather.3.cloned.1.call-done) | data formatting | bytes 15728640 | tf_op jit(solution)/shard_map/convert_element_type | solution.py:75
  238.7 11.9 %reshape.109 = f32[640,4096]{1,0:T(8,128)} reshape(f32[64,10,4096]{2,1,0:T(8,128)} %copy.39) | data formatting | bytes 20971520 | tf_op jit(solution)/shard_map/convert_element_type | solution.py:75
  250.6 6.1 %multiply_reduce_fusion = f32[640]{0:T(1024)S(1)} fusion(f32[640,4096]{1,0:T(8,128)} %reshape.109, bf16[640,192]{0,1:T(8,128)(2,1)S(1)} %get-tuple-element.9, bf16[1,1,192,4096]{3,2,1,0:T(8,128)(2,1)} %param.13), kind=kOutput, calls=%fused_computation.3 | convolution fusion | flops 1011875200 | bytes 12306944 | tf_op jit(solution)/shard_map/dot_general | solution.py:74
  256.7 0.8 reshape.105
  257.5 16.4 %reduce-scatter.3.cloned.1.call-done = f32[1,16,10]{2,1,0:T(8,128)} async-done(((f32[4,16,10]{2,1,0:T(8,128)}), f32[1,16,10]{2,1,0:T(8,128)}) %reduce-scatter.3.cloned.1.call-update) | async-done | bytes 656 | tf_op jit(solution)/shard_map/reduce_scatter | solution.py:76
  273.9 9.9 %all-to-all-start.3 = ((f32[16,1,10]{2,1,0:T(1,128)}), f32[16,1,10]{2,1,0:T(1,128)S(1)}, u32[]{:S(2)}, u32[]{:S(2)}) async-start(f32[16,1,10]{2,1,0:T(1,128)} %bitcast.66), calls=%async_computation.4 | async-start | bytes 16384 | tf_op jit(solution)/shard_map/all_to_all | solution.py:79
  284.1 6.7 %all-to-all-done.3 = f32[16,1,10]{2,1,0:T(1,128)S(1)} async-done(((f32[16,1,10]{2,1,0:T(1,128)}), f32[16,1,10]{2,1,0:T(1,128)S(1)}, u32[]{:S(2)}, u32[]{:S(2)}) %all-to-all-start.3) | async-done | bytes 672 | tf_op jit(solution)/shard_map/all_to_all | solution.py:79
  291.4 0.7 reduce.4
  292.4 10.1 %all_to_all.40 = bf16[16,1,10]{2,1,0:T(2,128)(2,1)S(1)} all-to-all(bf16[16,1,10]{2,1,0:T(2,128)(2,1)S(1)} %convert_element_type.125), channel_id=1, replica_groups=mesh['pipe'=4,'expert'=16,'dp'=4] {'expert'}, dimensions={0} | all-to-all | bytes 640 | tf_op jit(solution)/shard_map/all_to_all | solution.py:61
  302.5 9.0 %all-gather = bf16[64,1,10]{2,0,1:T(8,128)(2,1)S(1)} all-gather(bf16[16,1,10]{2,0,1:T(8,128)(2,1)S(1)} %copy.42), channel_id=2, replica_groups=mesh['pipe'=4,'expert'=16,'dp'=4] {'dp'}, dimensions={0}, use_global_device_ids=true | all-gather | bytes 1600 | tf_op jit(solution)/shard_map/all_gather | solution.py:64
  311.6 4.5 multiply_convert_fusion.1
  316.1 6.4 %copy.44 = bf16[64,10,4096]{2,1,0:T(8,128)(2,1)} copy(bf16[64,10,4096]{2,0,1:T(8,128)(2,1)S(1)} %multiply_convert_fusion.1) | data formatting | bytes 10485760 | tf_op jit(solution)/shard_map/convert_element_type | solution.py:65
  322.6 8.6 %convert_element_type.110 = bf16[640,4096]{1,0:T(8,128)(2,1)} reshape(bf16[64,10,4096]{2,1,0:T(8,128)(2,1)} %copy.44) | data formatting | bytes 10485760 | tf_op jit(solution)/shard_map/convert_element_type | solution.py:65
  331.2 5.0 multiply_convert_fusion.7
  336.3 1.6 fusion.12
  337.8 4.0 add_convert_fusion
  341.9 8.2 %reshape.106 = bf16[4,16,10,4096]{3,2,1,0:T(8,128)(2,1)} reshape(bf16[640,4096]{1,0:T(8,128)(2,1)} %add_convert_fusion) | data formatting | bytes 10485760 | tf_op jit(solution)/shard_map/reshape | solution.py:101
  350.1 80.8 %reduce-scatter.5.cloned.1.call-done = bf16[1,16,10,4096]{3,2,1,0:T(8,128)(2,1)} async-done(((bf16[4,16,10,4096]{3,2,1,0:T(8,128)(2,1)}), bf16[1,16,10,4096]{3,2,1,0:T(8,128)(2,1)}) %reduce-scatter.5.cloned.1.call-update) | async-done | bytes 1310736 | tf_op jit(solution)/shard_map/reduce_scatter | solution.py:102
  430.9 7.6 %all-to-all-start.5 = ((bf16[16,10,4096]{2,1,0:T(8,128)(2,1)}), bf16[16,10,4096]{2,1,0:T(8,128)(2,1)}, u32[]{:S(2)}, u32[]{:S(2)}) async-start(bf16[16,10,4096]{2,1,0:T(8,128)(2,1)} %bitcast.64), calls=%async_computation.7 | async-start | bytes 4194304 | tf_op jit(solution)/shard_map/all_to_all | solution.py:104
  438.5 0.7 subtract_multiply_fusion
  439.2 48.4 %all-to-all-done.5 = bf16[16,10,4096]{2,1,0:T(8,128)(2,1)} async-done(((bf16[16,10,4096]{2,1,0:T(8,128)(2,1)}), bf16[16,10,4096]{2,1,0:T(8,128)(2,1)}, u32[]{:S(2)}, u32[]{:S(2)}) %all-to-all-start.5) | async-done | bytes 1310752 | tf_op jit(solution)/shard_map/all_to_all | solution.py:104
  487.6 1.8 reshape.108
  489.4 1.5 convolution_convert_fusion.4
  490.8 1.7 collective-permute-start
  492.5 5.0 fusion.4
  497.7 5.0 fusion.5
  502.7 6.6 %fusion.3 = bf16[1,1,192,4096]{3,2,1,0:T(8,128)(2,1)} fusion(bf16[640,192]{0,1:T(8,128)(2,1)S(1)} %get-tuple-element.9, f32[640,4096]{1,0:T(8,128)} %reshape.109, f32[640]{0:T(1024)S(1)} %reshape.110), kind=kOutput, calls=%fused_computation.12 | convolution fusion | flops 1012662272 | bytes 12306944 | tf_op jit(solution)/shard_map/dot_general | solution.py:90
  509.3 8.2 %collective-permute-done = bf16[128,4096]{1,0:T(8,128)(2,1)S(1)} collective-permute-done((bf16[128,4096]{1,0:T(8,128)(2,1)}, bf16[128,4096]{1,0:T(8,128)(2,1)S(1)}, u32[]{:S(2)}, u32[]{:S(2)}) %collective-permute-start) | collective-permute-done | bytes 1048608 | tf_op jit(solution)/shard_map/ppermute | solution.py:17
  517.5 1.0 copy.46
  (39 shorter events, 1.9 us)
Async XLA Ops:
  7.2 217.8 %copy-start = (bf16[1,1,192,4096]{3,2,1,0:T(8,128)(2,1)S(1)}, bf16[1,1,192,4096]{3,2,1,0:T(8,128)(2,1)}, u32[]{:S(2)}) copy-start(bf16[1,1,192,4096]{3,2,1,0:T(8,128)(2,1)} %param.12) | copy-start | bytes 4718596
  7.2 219.7 %all-gather.3.cloned.1.call-start = ((), (), s32[]{:S(2)}) async-start(), calls=%async_computation.8 | async-start | bytes 6553600 | tf_op jit(solution)/shard_map/all_gather | solution.py:63
  136.7 5.5 %copy-start.6 = (f32[1,128,8]{1,2,0:T(8,128)S(1)}, f32[1,128,8]{1,2,0:T(8,128)}, u32[]{:S(2)}) copy-start(f32[1,128,8]{1,2,0:T(8,128)} %param.9) | copy-start | bytes 12292
  136.7 65.0 %all-to-all-start.1 = ((bf16[4,16,10,4096]{3,1,2,0:T(8,128)(2,1)}), bf16[4,16,10,4096]{3,1,2,0:T(8,128)(2,1)}, u32[]{:S(2)}, u32[]{:S(2)}) async-start(bf16[4,16,10,4096]{3,1,2,0:T(8,128)(2,1)} %stack.2), calls=%async_computation.1 | async-start | bytes 10485760 | tf_op jit(solution)/shard_map/all_to_all | solution.py:10
  142.0 131.9 %reduce-scatter.3.cloned.1.call-start = ((), (), s32[]{:S(2)}) async-start(), calls=%async_computation.9 | async-start | bytes 40960 | tf_op jit(solution)/shard_map/reduce_scatter | solution.py:76
  210.9 8.8 %copy-start.4 = (bf16[1,1,192,4096]{3,2,1,0:T(8,128)(2,1)S(1)}, bf16[1,1,192,4096]{3,2,1,0:T(8,128)(2,1)}, u32[]{:S(2)}) copy-start(bf16[1,1,192,4096]{3,2,1,0:T(8,128)(2,1)} %param.11) | copy-start | bytes 4718596
  219.6 5.3 %copy-start.1 = (bf16[640,4096]{1,0:T(8,128)(2,1)S(1)}, bf16[640,4096]{1,0:T(8,128)(2,1)}, u32[]{:S(2)}) copy-start(bf16[640,4096]{1,0:T(8,128)(2,1)} %reshape_reshape.3) | copy-start | bytes 15728644
  224.2 0.8 copy-start.7
  273.9 16.9 %all-to-all-start.3 = ((f32[16,1,10]{2,1,0:T(1,128)}), f32[16,1,10]{2,1,0:T(1,128)S(1)}, u32[]{:S(2)}, u32[]{:S(2)}) async-start(f32[16,1,10]{2,1,0:T(1,128)} %bitcast.66), calls=%async_computation.4 | async-start | bytes 16384 | tf_op jit(solution)/shard_map/all_to_all | solution.py:79
  283.8 147.0 %reduce-scatter.5.cloned.1.call-start = ((), (), s32[]{:S(2)}) async-start(), calls=%async_computation.10 | async-start | bytes 10485760 | tf_op jit(solution)/shard_map/reduce_scatter | solution.py:102
  322.6 8.6 %copy-start.8 = (f32[640,192]{0,1:T(8,128)S(1)}, f32[640,192]{0,1:T(8,128)}, u32[]{:S(2)}) copy-start(f32[640,192]{0,1:T(8,128)} %copy-done.7) | copy-start | bytes 1474564
  331.2 5.0 copy-start.5
  336.2 1.6 copy-start.2
  430.9 56.7 %all-to-all-start.5 = ((bf16[16,10,4096]{2,1,0:T(8,128)(2,1)}), bf16[16,10,4096]{2,1,0:T(8,128)(2,1)}, u32[]{:S(2)}, u32[]{:S(2)}) async-start(bf16[16,10,4096]{2,1,0:T(8,128)(2,1)} %bitcast.64), calls=%async_computation.7 | async-start | bytes 4194304 | tf_op jit(solution)/shard_map/all_to_all | solution.py:104
  490.8 6.9 %copy-start.3 = (bf16[640,192]{0,1:T(8,128)(2,1)S(1)}, bf16[640,192]{0,1:T(8,128)(2,1)}, u32[]{:S(2)}) copy-start(bf16[640,192]{0,1:T(8,128)(2,1)} %copy-done.2) | copy-start | bytes 737284
  490.8 26.6 %collective-permute-start = (bf16[128,4096]{1,0:T(8,128)(2,1)}, bf16[128,4096]{1,0:T(8,128)(2,1)S(1)}, u32[]{:S(2)}, u32[]{:S(2)}) collective-permute-start(bf16[128,4096]{1,0:T(8,128)(2,1)} %convolution_convert_fusion.4), channel_id=1, source_target_pairs={{64,0},{128,64},{192,128},{65,1},{129,65},{193,129},{66,2},{130,66... | collective-permute-start | bytes 3145736 | tf_op jit(solution)/shard_map/ppermute | solution.py:17
Sparse Core Ops, SparseCore 0:
  76.0 56.2 all-gather.2
  257.6 16.2 reduce-scatter.2
  350.2 80.6 reduce-scatter.4
